TPU v7x, 32 devices: a whole 2x2x4 slice. The times are simulated.
32 devices in a mesh: axial: 8 (over y, x, core), radial: 4 (over z).
Axes of the slice: x: 2, y: 2, z: 4, core: 2. Of those that a mesh axis runs over, the one named last changes fastest.
Arguments:
- composition_deviations: float32 [38, 1024, 512], P(None, 'axial', 'radial'), may hold values from -6 to 6
- flow_speed_vector: float32 [2, 1024, 512], P(None, 'axial', 'radial'), may hold values from -1 to 1
- thermal_field: float32 [1024, 512], P('axial', 'radial'), may hold values from 0.4 to 4
- linearized_kinetics_operator: float32 [38, 38], replicated, may hold values from -0.5 to 0.5
- frozen_jacobian_inverse_addend: float32 [38, 38], replicated, may hold values from -0.25 to 0.25
- rigid_block_indicator: int32 [512, 4], P('axial', 'radial'), may hold values from 0 to 1, as said below
- molar_absorptivity_table: float32 [4, 38], replicated, may hold values from -1 to 1
- spokewise_sightline_length: float32 [512], P('radial'), may hold values from 0.3 to 3
- sightline_lengthwise_index: int32 [4, 32768], replicated, may hold values from 0 to 1023
- observed_absorbance_traces: float32 [4, 32768], P(None, ('axial', 'radial')), may hold values from -6 to 6
Outputs:
- species_out: float32 [38, 1024, 512], P(None, 'axial', 'radial')
- misfit: float32 [4, 32768], P(None, ('axial', 'radial'))
Inputs may be any that keep to these rules, and one draw needn't show every extreme that they name: `rigid_block_indicator`: in each radial column of tiles, the tiles of 2 cyclically consecutive axial devices are all stiff and every other axial device holds exactly 8 stiff tiles, so the column holds 176 stiff tiles.
All inputs are finite; a program needn't handle non-finite values.
Results may differ from a plain program's by a relative error of at most 0.0001.
Values sent between devices are 32-bit elements; how exact they have to be, the bound alone decides.
No kernel may reach another device: no remote copies, remote signals or barrier semaphores. Data moves between devices by JAX's collectives and lax.ppermute only.
A program may use at most 192 MiB of HBM per device.

v0:
```python
import math
import jax
import jax.numpy as jnp
from jax import lax
from jax.sharding import PartitionSpec as P

TILE_ROWS = 2
ITERS = 3
TIME_STEP = 0.4
CHEM_STEP = 0.5
ARRHENIUS_BARRIER = 1.0
WENO_EPS = 1e-06
HIGHEST = lax.Precision.HIGHEST


def extended(shard, sides, width):
    for axis, dim in sides:
        peers, length = (lax.axis_size(axis), shard.shape[dim])
        up = [(i, (i + 1) % peers) for i in range(peers - 1)]
        down = [(j, i) for i, j in up]
        last = lax.slice_in_dim(shard, length - width, length, axis=dim)
        initial = lax.slice_in_dim(shard, 0, width, axis=dim)
        before = lax.ppermute(last, axis, up)
        after = lax.ppermute(initial, axis, down)
        shard = jnp.concatenate([before, shard, after], axis=dim)
    return shard


def weno_side(minus_two, minus_one, centre, plus_one, plus_two):
    beta_zero = (
        13.0 / 12.0 * (minus_two - 2.0 * minus_one + centre) ** 2
        + 0.25 * (minus_two - 4.0 * minus_one + 3.0 * centre) ** 2
    )
    beta_one = (
        13.0 / 12.0 * (minus_one - 2.0 * centre + plus_one) ** 2
        + 0.25 * (minus_one - plus_one) ** 2
    )
    beta_two = (
        13.0 / 12.0 * (centre - 2.0 * plus_one + plus_two) ** 2
        + 0.25 * (3.0 * centre - 4.0 * plus_one + plus_two) ** 2
    )
    weight_zero = 0.1 / (WENO_EPS + beta_zero) ** 2
    weight_one = 0.6 / (WENO_EPS + beta_one) ** 2
    weight_two = 0.3 / (WENO_EPS + beta_two) ** 2
    weight_total = weight_zero + weight_one + weight_two
    blended = weight_zero * (2.0 * minus_two - 7.0 * minus_one + 11.0 * centre)
    blended = blended + weight_one * (-minus_one + 5.0 * centre + 2.0 * plus_one)
    blended = blended + weight_two * (2.0 * centre + 5.0 * plus_one - plus_two)
    return blended / (6.0 * weight_total)


def face_difference(field, speed, along, length):
    face_count = length + 1

    def cut_part(offset):
        return lax.slice_in_dim(field, offset, offset + face_count, axis=along)

    left_value = weno_side(cut_part(0), cut_part(1), cut_part(2), cut_part(3), cut_part(4))
    right_value = weno_side(cut_part(5), cut_part(4), cut_part(3), cut_part(2), cut_part(1))
    face_speed = 0.5 * (
        lax.slice_in_dim(speed, 2, 2 + face_count, axis=along)
        + lax.slice_in_dim(speed, 3, 3 + face_count, axis=along)
    )
    face_flux = (
        jnp.maximum(face_speed, 0.0) * left_value + jnp.minimum(face_speed, 0.0) * right_value
    )
    return lax.slice_in_dim(face_flux, 1, face_count, axis=along) - lax.slice_in_dim(
        face_flux, 0, face_count - 1, axis=along
    )


def transport(field_pad, speed_pad):
    row_count = field_pad.shape[1] - 6
    col_count = field_pad.shape[2] - 6
    along_axial = face_difference(field_pad[:, :, 3:-3], speed_pad[0:1, :, 3:-3], 1, row_count)
    along_radial = face_difference(field_pad[:, 3:-3, :], speed_pad[1:2, 3:-3, :], 2, col_count)
    return field_pad[:, 3:-3, 3:-3] - TIME_STEP * (along_axial + along_radial)


def kinetics_advance(
    starting_composition_field,
    thermal_field,
    linearized_kinetics_operator,
    frozen_jacobian_inverse_addend,
):
    acceleration_factor = jnp.exp(-ARRHENIUS_BARRIER / thermal_field)
    current = starting_composition_field
    for newton_step in range(ITERS):
        source = jnp.tensordot(
            linearized_kinetics_operator, current, axes=(1, 0), precision=HIGHEST
        ) - jnp.tanh(current)
        defect = current - starting_composition_field - CHEM_STEP * acceleration_factor * source
        current = (
            current
            - defect
            - jnp.tensordot(frozen_jacobian_inverse_addend, defect, axes=(1, 0), precision=HIGHEST)
        )
    return current


def absorbance_profile(field, molar_absorptivity_table, spokewise_sightline_length):
    mixed = jnp.tensordot(molar_absorptivity_table, field, axes=(1, 0), precision=HIGHEST)
    return jnp.dot(mixed, spokewise_sightline_length, precision=HIGHEST)


def local(
    composition_deviations,
    flow_speed_vector,
    thermal_field,
    linearized_kinetics_operator,
    frozen_jacobian_inverse_addend,
    rigid_block_indicator,
    molar_absorptivity_table,
    spokewise_sightline_length,
    sightline_lengthwise_index,
    observed_absorbance_traces,
):
    species_count = composition_deviations.shape[0]
    stacked = jnp.concatenate([composition_deviations, flow_speed_vector], axis=0)
    padded = extended(stacked, (("axial", 1), ("radial", 2)), 3)
    advected_composition_field = transport(padded[:species_count], padded[species_count:])
    combusted_composition_field = kinetics_advance(
        advected_composition_field,
        thermal_field,
        linearized_kinetics_operator,
        frozen_jacobian_inverse_addend,
    )
    flag_cells = jnp.repeat(
        jnp.repeat(rigid_block_indicator, TILE_ROWS, axis=0),
        advected_composition_field.shape[2],
        axis=1,
    )
    species_out = jnp.where(
        flag_cells[None] > 0, combusted_composition_field, advected_composition_field
    )
    path_scale = 1.0 / math.sqrt(advected_composition_field.shape[2] * lax.axis_size("radial"))
    profile = (
        absorbance_profile(species_out, molar_absorptivity_table, spokewise_sightline_length)
        * path_scale
    )
    column = lax.psum(profile, "radial")
    whole_profile = lax.all_gather(column, "axial", axis=1, tiled=True)
    device = lax.axis_index(("axial", "radial"))
    sample_count = observed_absorbance_traces.shape[1]
    own_rows = lax.dynamic_slice_in_dim(
        sightline_lengthwise_index, device * sample_count, sample_count, 1
    )
    values = jnp.take_along_axis(whole_profile, own_rows, axis=1)
    return (species_out, values - observed_absorbance_traces)


def solution(mesh):
    in_specs = (
        P(None, "axial", "radial"),
        P(None, "axial", "radial"),
        P("axial", "radial"),
        P(),
        P(),
        P("axial", "radial"),
        P(),
        P("radial"),
        P(),
        P(None, ("axial", "radial")),
    )
    out_specs = (P(None, "axial", "radial"), P(None, ("axial", "radial")))
    return jax.shard_map(local, mesh=mesh, in_specs=in_specs, out_specs=out_specs, check_vma=False)
```

profile of v0, /device:TPU:0, one launch (start us, length us, event | category | flops | bytes accessed | tf_op | source)
XLA Modules:
  0.0 168.7 jit_solution(240044641915545838)
XLA Ops:
  0.7 2.6 %copy.75 = f32[38,128,128]{1,0,2:T(8,128)S(1)} copy(f32[38,128,128]{2,1,0:T(8,128)} %param.10) | data formatting | bytes 4980736 | tf_op args[0]
  3.4 3.3 %slice_maximum_fusion = (f32[40,3,128]{1,0,2:T(8,128)}, f32[40,3,128]{1,0,2:T(8,128)}) fusion(f32[2,128,128]{1,0,2:T(2,128)S(1)} %copy.64, f32[38,128,128]{1,0,2:T(8,128)S(1)} %copy.75), kind=kLoop, calls=%fused_computation.63 | loop fusion | flops 30720 | bytes 2744320 | tf_op jit(solution)/shard_map/concatenate | solution.py:119
  6.7 2.5 %copy.67 = f32[40,3,128]{2,0,1:T(8,128)S(1)} copy(f32[40,3,128]{1,0,2:T(8,128)} %get-tuple-element.25) | data formatting | bytes 122880 | tf_op jit(solution)/shard_map/slice | solution.py:22
  9.2 1.3 collective-permute-start.1
  10.5 2.5 %copy.65 = f32[40,3,128]{2,0,1:T(8,128)S(1)} copy(f32[40,3,128]{1,0,2:T(8,128)} %get-tuple-element.24) | data formatting | bytes 122880 | tf_op jit(solution)/shard_map/slice | solution.py:21
  13.1 3.0 %collective-permute-start = (f32[40,3,128]{2,0,1:T(8,128)S(1)}, f32[40,3,128]{2,0,1:T(8,128)S(1)}, u32[]{:S(2)}, u32[]{:S(2)}) collective-permute-start(f32[40,3,128]{2,0,1:T(8,128)S(1)} %copy.65), channel_id=1, source_target_pairs={{0,4},{4,8},{8,12},{12,16},{16,20},{20,24},{24,28},{1,5},{5,9},{9,... | collective-permute-start | bytes 184328 | tf_op jit(solution)/shard_map/ppermute | solution.py:23
  16.5 0.7 fusion.80
  17.3 2.3 %copy.68 = f32[40,3,128]{1,0,2:T(8,128)} copy(f32[40,3,128]{2,0,1:T(8,128)S(1)} %collective-permute-done.1) | data formatting | bytes 122880 | tf_op jit(solution)/shard_map/ppermute | solution.py:24
  19.6 2.3 %copy.66 = f32[40,3,128]{1,0,2:T(8,128)} copy(f32[40,3,128]{2,0,1:T(8,128)S(1)} %collective-permute-done) | data formatting | bytes 122880 | tf_op jit(solution)/shard_map/ppermute | solution.py:23
  21.9 1.2 pad_maximum_fusion.6
  23.1 0.6 copy-done.1
  23.7 0.8 copy-done.2
  24.5 2.7 %maximum_maximum_fusion.1 = (f32[40,131,128]{1,0,2:T(8,128)S(1)}, f32[40,131,128]{1,0,2:T(8,128)S(1)}) fusion(f32[2,128,128]{1,0,2:T(2,128)S(1)} %copy.64, f32[38,128,128]{1,0,2:T(8,128)S(1)} %copy.75, f32[40,3,128]{1,0,2:T(8,128)S(1)} %copy-done.2, f32[40,3,128]{1,0,2:T(8,128)S(1)} %copy-done.1), kind=kLoop, calls=%fused_computation.3 | loop fusion | flops 2682880 | bytes 8110080 | tf_op jit(solution)/shard_map/concatenate | solution.py:25
  27.2 0.8 broadcast_maximum_fusion
  28.0 4.9 %collective-permute-start.2 = (f32[40,134,3]{1,0,2:T(8,128)S(1)}, f32[40,134,3]{1,0,2:T(8,128)S(1)}, u32[]{:S(2)}, u32[]{:S(2)}) collective-permute-start(f32[40,134,3]{1,0,2:T(8,128)S(1)} %get-tuple-element.20), channel_id=1, source_target_pairs={{0,1},{1,2},{2,3},{4,5},{5,6},{6,7},{8,9},{9,10},{10,11},{12,13},{... | collective-permute-start | bytes 192968 | tf_op jit(solution)/shard_map/ppermute | solution.py:23
  32.9 1.5 collective-permute-start.3
  34.5 25.3 %multiply_add_fusion = f32[38,129,128]{1,0,2:T(8,128)} fusion(f32[40,131,128]{1,0,2:T(8,128)S(1)} %get-tuple-element.23, f32[40,131,128]{1,0,2:T(8,128)S(1)} %get-tuple-element.22, f32[129,128]{0,1:T(8,128)S(1)} %get-tuple-element.28, f32[129,128]{0,1:T(8,128)S(1)} %get-tuple-element.29), kind=kLoop, calls=%fused_computation.5 | loop fusion | flops 77177088 | bytes 17700864 | tf_op jit(solution)/shard_map/add | solution.py:65
  60.2 7.2 %maximum_maximum_fusion = (f32[40,134,131]{1,0,2:T(8,128)S(1)}, f32[40,134,131]{1,0,2:T(8,128)S(1)}) fusion(f32[40,3,128]{1,0,2:T(8,128)S(1)} %copy-done.1, f32[2,128,128]{1,0,2:T(2,128)S(1)} %copy.64, f32[38,128,128]{1,0,2:T(8,128)S(1)} %copy.75, f32[40,3,128]{1,0,2:T(8,128)S(1)} %copy-done.2, f32[40,134,3]{1,0,2:T(8,128)S(1)} %collective-permute-done.2, ...), kind=kLoop, calls=%fused_computation.1 | loop fusion | flops 5617280 | bytes 8490240 | tf_op jit(solution)/shard_map/concatenate | solution.py:25
  67.4 13.0 %multiply_add_fusion.3 = f32[38,128,129]{1,0,2:T(8,128)S(1)} fusion(f32[40,134,131]{1,0,2:T(8,128)S(1)} %get-tuple-element.19, f32[40,134,131]{1,0,2:T(8,128)S(1)} %get-tuple-element.18, f32[128,129]{0,1:T(8,128)S(1)} %get-tuple-element.26, f32[128,129]{0,1:T(8,128)S(1)} %get-tuple-element.27), kind=kLoop, calls=%fused_computation.31 | loop fusion | flops 77177088 | bytes 17700864 | tf_op jit(solution)/shard_map/add | solution.py:65
  80.5 4.3 %fusion.44 = f32[38,128,128]{1,0,2:T(8,128)S(1)} fusion(f32[38,128,128]{1,0,2:T(8,128)S(1)} %copy.75, f32[38,128,129]{1,0,2:T(8,128)S(1)} %multiply_add_fusion.3, f32[38,129,128]{1,0,2:T(8,128)} %multiply_add_fusion), kind=kLoop, calls=%fused_computation.60 | loop fusion | flops 3112960 | bytes 14942208 | tf_op jit(solution)/shard_map/sub | solution.py:77
  84.8 2.5 %fusion.78 = f32[128,128,38]{0,2,1:T(8,128)S(1)} fusion(f32[38,128,128]{1,0,2:T(8,128)S(1)} %fusion.44, f32[38,38]{1,0:T(8,128)S(1)} %copy-done), kind=kOutput, calls=%fused_computation.113 | convolution fusion | flops 283901952 | bytes 4986512 | tf_op jit(solution)/shard_map/dot_general | solution.py:89
  87.3 4.1 %bitcast_subtract_fusion.4 = f32[38,128,128]{1,0,2:T(8,128)S(1)} fusion(f32[38,128,128]{1,0,2:T(8,128)S(1)} %fusion.44, f32[128,128,38]{0,2,1:T(8,128)S(1)} %fusion.78, f32[128,128]{0,1:T(8,128)S(1)} %copy.76, f32[38,38]{1,0:T(8,128)S(1)} %copy-done.4), kind=kOutput, calls=%fused_computation.73 | convolution fusion | flops 290127872 | bytes 7542416 | tf_op jit(solution)/shard_map/dot_general | solution.py:96
  91.4 2.4 %fusion.76 = f32[128,128,38]{0,2,1:T(8,128)S(1)} fusion(f32[38,128,128]{1,0,2:T(8,128)S(1)} %bitcast_subtract_fusion.4, f32[38,38]{1,0:T(8,128)S(1)} %copy-done), kind=kOutput, calls=%fused_computation.111 | convolution fusion | flops 283901952 | bytes 4986512 | tf_op jit(solution)/shard_map/dot_general | solution.py:89
  93.8 4.5 %bitcast_subtract_fusion.2 = f32[38,128,128]{1,0,2:T(8,128)S(1)} fusion(f32[38,128,128]{1,0,2:T(8,128)S(1)} %bitcast_subtract_fusion.4, f32[128,128,38]{0,2,1:T(8,128)S(1)} %fusion.76, f32[38,128,128]{1,0,2:T(8,128)S(1)} %fusion.44, f32[128,128]{0,1:T(8,128)S(1)} %copy.76, f32[38,38]{1,0:T(8,128)S(1)} %copy-done.4), kind=kOutput, calls=%fused_computation.69 | convolution fusion | flops 290127872 | bytes 10032784 | tf_op jit(solution)/shard_map/dot_general | solution.py:96
  98.3 2.3 %fusion.74 = f32[128,128,38]{0,2,1:T(8,128)S(1)} fusion(f32[38,128,128]{1,0,2:T(8,128)S(1)} %bitcast_subtract_fusion.2, f32[38,38]{1,0:T(8,128)S(1)} %copy-done), kind=kOutput, calls=%fused_computation.109 | convolution fusion | flops 283901952 | bytes 4986512 | tf_op jit(solution)/shard_map/dot_general | solution.py:89
  100.6 4.4 %fusion.45 = f32[38,128,128]{1,0,2:T(8,128)S(1)} fusion(f32[38,128,128]{1,0,2:T(8,128)S(1)} %fusion.44, f32[38,128,128]{1,0,2:T(8,128)S(1)} %bitcast_subtract_fusion.2, f32[128,128,38]{0,2,1:T(8,128)S(1)} %fusion.74, f32[128,128]{0,1:T(8,128)S(1)} %copy.76, pred[128]{0:T(512)(128)(4,1)S(1)} %gt.22, f32[38,38]{1,0:T(8,128)S(1)} %copy-done.4), kind=kOutput, calls=%fused_computation.65 | convolution fusion | flops 290750464 | bytes 10032912 | tf_op jit(solution)/shard_map/dot_general | solution.py:96
  104.9 2.1 %copy.77 = f32[38,128,128]{2,1,0:T(8,128)} copy(f32[38,128,128]{1,0,2:T(8,128)S(1)} %fusion.45) | data formatting | bytes 4980736
  107.1 1.7 %convolution_bitcast_fusion = f32[4,128,128]{1,0,2:T(4,128)S(1)} fusion(f32[38,128,128]{1,0,2:T(8,128)S(1)} %fusion.45, f32[4,38]{1,0:T(4,128)S(1)} %copy-done.7), kind=kOutput, calls=%fused_computation.85 | convolution fusion | flops 29884416 | bytes 2753120 | tf_op jit(solution)/shard_map/dot_general | solution.py:102
  109.1 13.0 %psum.7 = f32[4,128]{1,0:T(4,128)S(1)} all-reduce(f32[4,128]{1,0:T(4,128)S(1)} %broadcast_multiply_fusion), channel_id=1, replica_groups=mesh['axial'=8,'radial'=4] {'radial'}, use_global_device_ids=true, to_apply=%region_0.1 | all-reduce | flops 512 | bytes 4096 | tf_op jit(solution)/shard_map/psum | solution.py:141
  122.1 10.3 %all_gather.3 = f32[4,1024]{1,0:T(4,128)S(1)} all-gather(f32[4,128]{1,0:T(4,128)S(1)} %psum.7), channel_id=1, replica_groups=mesh['axial'=8,'radial'=4] {'axial'}, dimensions={1}, use_global_device_ids=true | all-gather | bytes 18432 | tf_op jit(solution)/shard_map/all_gather | solution.py:142
  132.4 35.0 %gather_fusion = f32[4096]{0:T(1024)S(1)} fusion(f32[4,1024]{1,0:T(4,128)S(1)} %all_gather.3, s32[4096]{0:T(1024)S(1)} %bitcast.92), kind=kCustom, calls=%fused_computation | custom fusion | bytes 65536 | tf_op jit(solution)/shard_map/jit(take_along_axis)/gather | solution.py:148
  167.4 1.3 select_subtract_fusion
  (37 shorter events, 1.4 us)
Async XLA Ops:
  0.6 84.1 %copy-start = (f32[38,38]{1,0:T(8,128)S(1)}, f32[38,38]{1,0:T(8,128)}, u32[]{:S(2)}) copy-start(f32[38,38]{1,0:T(8,128)} %param.13) | copy-start | bytes 17332
  0.6 2.6 %copy-start.3 = (f32[2,128,128]{2,1,0:T(8,128)S(1)}, f32[2,128,128]{2,1,0:T(8,128)}, u32[]{:S(2)}) copy-start(f32[2,128,128]{2,1,0:T(8,128)} %param.11) | copy-start | bytes 393220
  6.7 9.4 %copy-start.5 = (f32[128,128]{1,0:T(8,128)S(1)}, f32[128,128]{1,0:T(8,128)}, u32[]{:S(2)}) copy-start(f32[128,128]{1,0:T(8,128)} %param.12) | copy-start | bytes 196612
  6.7 9.6 %copy-start.9 = (s32[64,1]{0,1:T(1,128)S(1)}, s32[64,1]{0,1:T(1,128)}, u32[]{:S(2)}) copy-start(s32[64,1]{0,1:T(1,128)} %param.15) | copy-start | bytes 772
  9.2 8.0 %collective-permute-start.1 = (f32[40,3,128]{2,0,1:T(8,128)S(1)}, f32[40,3,128]{2,0,1:T(8,128)S(1)}, u32[]{:S(2)}, u32[]{:S(2)}) collective-permute-start(f32[40,3,128]{2,0,1:T(8,128)S(1)} %copy.67), channel_id=1, source_target_pairs={{4,0},{8,4},{12,8},{16,12},{20,16},{24,20},{28,24},{5,1},{9,5},{13... | collective-permute-start | bytes 184328 | tf_op jit(solution)/shard_map/ppermute | solution.py:24
  13.1 6.5 %collective-permute-start = (f32[40,3,128]{2,0,1:T(8,128)S(1)}, f32[40,3,128]{2,0,1:T(8,128)S(1)}, u32[]{:S(2)}, u32[]{:S(2)}) collective-permute-start(f32[40,3,128]{2,0,1:T(8,128)S(1)} %copy.65), channel_id=1, source_target_pairs={{0,4},{4,8},{8,12},{12,16},{16,20},{20,24},{24,28},{1,5},{5,9},{9,... | collective-permute-start | bytes 184328 | tf_op jit(solution)/shard_map/ppermute | solution.py:23
  21.9 1.9 %copy-start.1 = (f32[40,3,128]{1,0,2:T(8,128)S(1)}, f32[40,3,128]{1,0,2:T(8,128)}, u32[]{:S(2)}) copy-start(f32[40,3,128]{1,0,2:T(8,128)} %copy.68) | copy-start | bytes 184324
  21.9 2.6 %copy-start.2 = (f32[40,3,128]{1,0,2:T(8,128)S(1)}, f32[40,3,128]{1,0,2:T(8,128)}, u32[]{:S(2)}) copy-start(f32[40,3,128]{1,0,2:T(8,128)} %copy.66) | copy-start | bytes 184324
  28.0 31.9 %collective-permute-start.2 = (f32[40,134,3]{1,0,2:T(8,128)S(1)}, f32[40,134,3]{1,0,2:T(8,128)S(1)}, u32[]{:S(2)}, u32[]{:S(2)}) collective-permute-start(f32[40,134,3]{1,0,2:T(8,128)S(1)} %get-tuple-element.20), channel_id=1, source_target_pairs={{0,1},{1,2},{2,3},{4,5},{5,6},{6,7},{8,9},{9,10},{10,11},{12,13},{... | collective-permute-start | bytes 192968 | tf_op jit(solution)/shard_map/ppermute | solution.py:23
  32.9 26.9 %collective-permute-start.3 = (f32[40,134,3]{1,0,2:T(8,128)S(1)}, f32[40,134,3]{1,0,2:T(8,128)S(1)}, u32[]{:S(2)}, u32[]{:S(2)}) collective-permute-start(f32[40,134,3]{1,0,2:T(8,128)S(1)} %get-tuple-element.21), channel_id=1, source_target_pairs={{1,0},{2,1},{3,2},{5,4},{6,5},{7,6},{9,8},{10,9},{11,10},{13,12},{... | collective-permute-start | bytes 192968 | tf_op jit(solution)/shard_map/ppermute | solution.py:24
  84.8 2.5 %copy-start.4 = (f32[38,38]{1,0:T(8,128)S(1)}, f32[38,38]{1,0:T(8,128)}, u32[]{:S(2)}) copy-start(f32[38,38]{1,0:T(8,128)} %param.14) | copy-start | bytes 17332
  104.9 2.1 %copy-start.7 = (f32[4,38]{1,0:T(4,128)S(1)}, f32[4,38]{1,0:T(4,128)}, u32[]{:S(2)}) copy-start(f32[4,38]{1,0:T(4,128)} %param.16) | copy-start | bytes 1828
  107.1 1.7 %copy-start.8 = (f32[128]{0:T(128)S(1)}, f32[128]{0:T(128)}, u32[]{:S(2)}) copy-start(f32[128]{0:T(128)} %param.17) | copy-start | bytes 1540
  132.4 35.0 %copy-start.6 = (f32[4,1024]{1,0:T(4,128)S(1)}, f32[4,1024]{1,0:T(4,128)}, u32[]{:S(2)}) copy-start(f32[4,1024]{1,0:T(4,128)} %param.19) | copy-start | bytes 49156
where the time goes:
time: 169 us
  other arithmetic  60.4 us (36%)
  local copies, waits for them, and re-layouts  51.3 us (30%)
  blocking collectives  23.3 us (14%)
  matrix products  22.1 us (13%)
  starting transfers between devices  10.7 us (6%)
    add x2, other arithmetic, face_difference(): jnp.maximum(face_speed, 0.0) * left_value  38.3 us
    gather x2, local copies, waits for them, and re-layouts, local(): values = jnp.take_along_axis(whole_profile, own_rows, axis=1)  35 us
    psum x1, blocking collectives, local(): column = lax.psum(profile, 'radial')  13 us
    dot_general x3, matrix products, kinetics_advance(): jnp.tensordot(frozen_jacobian_inverse_addend, defect, axes=(1, 0), precis...  13 us
    all_gather x1, blocking collectives, local(): whole_profile = lax.all_gather(column, 'axial', axis=1, tiled=True)  10.3 us
    concatenate x2, other arithmetic, extended(): shard = jnp.concatenate([before, shard, after], axis=dim)  9.84 us
    ppermute x2, starting transfers between devices, extended(): before = lax.ppermute(last, axis, up)  7.97 us
    dot_general x3, matrix products, kinetics_advance(): jnp.tensordot(linearized_kinetics_operator, current, axes=(1, 0), precisi...  7.12 us
  transfers between devices with their start and end apart: 4, of which 0 were waited for; matrix products, arithmetic and copies ran while one was open for 19% of the time, Pallas kernels for 0%

commit v1 on v0

--- a/solution.py
+++ b/solution.py
@@ -139,7 +139,9 @@
         * path_scale
     )
     column = lax.psum(profile, "radial")
-    whole_profile = lax.all_gather(column, "axial", axis=1, tiled=True)
+    whole_profile = jnp.concatenate(
+        lax.all_to_all(jnp.stack([column] * lax.axis_size("axial")), "axial", 0, 0), axis=1
+    )
     device = lax.axis_index(("axial", "radial"))
     sample_count = observed_absorbance_traces.shape[1]
     own_rows = lax.dynamic_slice_in_dim(

time: 169 us -> 166 us (0.982)
  blocking collectives: 23.3 us -> 13 us
  starting transfers between devices: 10.7 us -> 15.7 us
  local copies, waits for them, and re-layouts: 51.3 us -> 53.2 us
    all_gather x1 -> x0, blocking collectives: 10.3 us -> none  [local(): whole_profile = lax.all_gather(column, 'axial', axis=1, tiled=True)]
    all_to_all x0 -> x1, starting transfers between devices: none -> 4.97 us  [local(): lax.all_to_all(jnp.stack([column] * lax.axis_size('axial')), 'axial', 0, 0)]
    unnamed x25 -> x27, local copies, waits for them, and re-layouts: 6.29 us -> 7.52 us
  transfers between devices with their start and end apart: 4 -> 5, of which waited for: 0 -> 1; matrix products, arithmetic and copies ran while one was open for 19% -> 21% of each run, Pallas kernels for 0% -> 0%
where the time goes in v1:
time: 166 us
  other arithmetic  60.4 us (36%)
  local copies, waits for them, and re-layouts  53.2 us (32%)
  matrix products  22.1 us (13%)
  starting transfers between devices  15.7 us (9%)
  blocking collectives  13 us (8%)
    add x2, other arithmetic, face_difference(): jnp.maximum(face_speed, 0.0) * left_value  38.3 us
    gather x2, local copies, waits for them, and re-layouts, local(): values = jnp.take_along_axis(whole_profile, own_rows, axis=1)  35 us
    psum x1, blocking collectives, local(): column = lax.psum(profile, 'radial')  13 us
    dot_general x3, matrix products, kinetics_advance(): jnp.tensordot(frozen_jacobian_inverse_addend, defect, axes=(1, 0), precis...  13 us
    concatenate x2, other arithmetic, extended(): shard = jnp.concatenate([before, shard, after], axis=dim)  9.84 us
    ppermute x2, starting transfers between devices, extended(): before = lax.ppermute(last, axis, up)  7.97 us
    unnamed x27, local copies, waits for them, and re-layouts  7.52 us
    dot_general x3, matrix products, kinetics_advance(): jnp.tensordot(linearized_kinetics_operator, current, axes=(1, 0), precisi...  7.12 us
  transfers between devices with their start and end apart: 5, of which 1 were waited for; matrix products, arithmetic and copies ran while one was open for 21% of the time, Pallas kernels for 0%

profile of v1, /device:TPU:0, one launch (start us, length us, event | category | flops | bytes accessed | tf_op | source)
XLA Modules:
  0.0 166.0 jit_solution(7243457039256928961)
XLA Ops:
  0.7 2.6 %copy.75 = f32[38,128,128]{1,0,2:T(8,128)S(1)} copy(f32[38,128,128]{2,1,0:T(8,128)} %param.10) | data formatting | bytes 4980736 | tf_op args[0]
  3.4 3.3 %slice_maximum_fusion = (f32[40,3,128]{1,0,2:T(8,128)}, f32[40,3,128]{1,0,2:T(8,128)}) fusion(f32[2,128,128]{1,0,2:T(2,128)S(1)} %copy.64, f32[38,128,128]{1,0,2:T(8,128)S(1)} %copy.75), kind=kLoop, calls=%fused_computation.63 | loop fusion | flops 30720 | bytes 2744320 | tf_op jit(solution)/shard_map/concatenate | solution.py:119
  6.7 2.5 %copy.67 = f32[40,3,128]{2,0,1:T(8,128)S(1)} copy(f32[40,3,128]{1,0,2:T(8,128)} %get-tuple-element.25) | data formatting | bytes 122880 | tf_op jit(solution)/shard_map/slice | solution.py:22
  9.3 1.3 collective-permute-start.1
  10.6 2.5 %copy.65 = f32[40,3,128]{2,0,1:T(8,128)S(1)} copy(f32[40,3,128]{1,0,2:T(8,128)} %get-tuple-element.24) | data formatting | bytes 122880 | tf_op jit(solution)/shard_map/slice | solution.py:21
  13.1 3.0 %collective-permute-start = (f32[40,3,128]{2,0,1:T(8,128)S(1)}, f32[40,3,128]{2,0,1:T(8,128)S(1)}, u32[]{:S(2)}, u32[]{:S(2)}) collective-permute-start(f32[40,3,128]{2,0,1:T(8,128)S(1)} %copy.65), channel_id=1, source_target_pairs={{0,4},{4,8},{8,12},{12,16},{16,20},{20,24},{24,28},{1,5},{5,9},{9,... | collective-permute-start | bytes 184328 | tf_op jit(solution)/shard_map/ppermute | solution.py:23
  16.5 2.3 %copy.68 = f32[40,3,128]{1,0,2:T(8,128)} copy(f32[40,3,128]{2,0,1:T(8,128)S(1)} %collective-permute-done.1) | data formatting | bytes 122880 | tf_op jit(solution)/shard_map/ppermute | solution.py:24
  18.8 2.3 %copy.66 = f32[40,3,128]{1,0,2:T(8,128)} copy(f32[40,3,128]{2,0,1:T(8,128)S(1)} %collective-permute-done) | data formatting | bytes 122880 | tf_op jit(solution)/shard_map/ppermute | solution.py:23
  21.2 1.2 pad_maximum_fusion.6
  23.0 0.8 copy-done.2
  23.8 2.7 %maximum_maximum_fusion.1 = (f32[40,131,128]{1,0,2:T(8,128)S(1)}, f32[40,131,128]{1,0,2:T(8,128)S(1)}) fusion(f32[2,128,128]{1,0,2:T(2,128)S(1)} %copy.64, f32[38,128,128]{1,0,2:T(8,128)S(1)} %copy.75, f32[40,3,128]{1,0,2:T(8,128)S(1)} %copy-done.2, f32[40,3,128]{1,0,2:T(8,128)S(1)} %copy-done.1), kind=kLoop, calls=%fused_computation.3 | loop fusion | flops 2682880 | bytes 8110080 | tf_op jit(solution)/shard_map/concatenate | solution.py:25
  26.5 0.8 broadcast_maximum_fusion
  27.3 4.9 %collective-permute-start.2 = (f32[40,134,3]{1,0,2:T(8,128)S(1)}, f32[40,134,3]{1,0,2:T(8,128)S(1)}, u32[]{:S(2)}, u32[]{:S(2)}) collective-permute-start(f32[40,134,3]{1,0,2:T(8,128)S(1)} %get-tuple-element.20), channel_id=1, source_target_pairs={{0,1},{1,2},{2,3},{4,5},{5,6},{6,7},{8,9},{9,10},{10,11},{12,13},{... | collective-permute-start | bytes 192968 | tf_op jit(solution)/shard_map/ppermute | solution.py:23
  32.2 1.5 collective-permute-start.3
  33.8 25.3 %multiply_add_fusion = f32[38,129,128]{1,0,2:T(8,128)} fusion(f32[40,131,128]{1,0,2:T(8,128)S(1)} %get-tuple-element.23, f32[40,131,128]{1,0,2:T(8,128)S(1)} %get-tuple-element.22, f32[129,128]{0,1:T(8,128)S(1)} %get-tuple-element.28, f32[129,128]{0,1:T(8,128)S(1)} %get-tuple-element.29), kind=kLoop, calls=%fused_computation.5 | loop fusion | flops 77177088 | bytes 17700864 | tf_op jit(solution)/shard_map/add | solution.py:65
  59.6 7.2 %maximum_maximum_fusion = (f32[40,134,131]{1,0,2:T(8,128)S(1)}, f32[40,134,131]{1,0,2:T(8,128)S(1)}) fusion(f32[40,3,128]{1,0,2:T(8,128)S(1)} %copy-done.1, f32[2,128,128]{1,0,2:T(2,128)S(1)} %copy.64, f32[38,128,128]{1,0,2:T(8,128)S(1)} %copy.75, f32[40,3,128]{1,0,2:T(8,128)S(1)} %copy-done.2, f32[40,134,3]{1,0,2:T(8,128)S(1)} %collective-permute-done.2, ...), kind=kLoop, calls=%fused_computation.1 | loop fusion | flops 5617280 | bytes 8490240 | tf_op jit(solution)/shard_map/concatenate | solution.py:25
  66.7 13.0 %multiply_add_fusion.3 = f32[38,128,129]{1,0,2:T(8,128)S(1)} fusion(f32[40,134,131]{1,0,2:T(8,128)S(1)} %get-tuple-element.19, f32[40,134,131]{1,0,2:T(8,128)S(1)} %get-tuple-element.18, f32[128,129]{0,1:T(8,128)S(1)} %get-tuple-element.26, f32[128,129]{0,1:T(8,128)S(1)} %get-tuple-element.27), kind=kLoop, calls=%fused_computation.31 | loop fusion | flops 77177088 | bytes 17700864 | tf_op jit(solution)/shard_map/add | solution.py:65
  79.8 4.3 %fusion.44 = f32[38,128,128]{1,0,2:T(8,128)S(1)} fusion(f32[38,128,128]{1,0,2:T(8,128)S(1)} %copy.75, f32[38,128,129]{1,0,2:T(8,128)S(1)} %multiply_add_fusion.3, f32[38,129,128]{1,0,2:T(8,128)} %multiply_add_fusion), kind=kLoop, calls=%fused_computation.60 | loop fusion | flops 3112960 | bytes 14942208 | tf_op jit(solution)/shard_map/sub | solution.py:77
  84.1 2.5 %fusion.78 = f32[128,128,38]{0,2,1:T(8,128)S(1)} fusion(f32[38,128,128]{1,0,2:T(8,128)S(1)} %fusion.44, f32[38,38]{1,0:T(8,128)S(1)} %copy-done), kind=kOutput, calls=%fused_computation.113 | convolution fusion | flops 283901952 | bytes 4986512 | tf_op jit(solution)/shard_map/dot_general | solution.py:89
  86.6 4.1 %bitcast_subtract_fusion.4 = f32[38,128,128]{1,0,2:T(8,128)S(1)} fusion(f32[38,128,128]{1,0,2:T(8,128)S(1)} %fusion.44, f32[128,128,38]{0,2,1:T(8,128)S(1)} %fusion.78, f32[128,128]{0,1:T(8,128)S(1)} %copy.76, f32[38,38]{1,0:T(8,128)S(1)} %copy-done.5), kind=kOutput, calls=%fused_computation.73 | convolution fusion | flops 290127872 | bytes 7542416 | tf_op jit(solution)/shard_map/dot_general | solution.py:96
  90.7 2.4 %fusion.76 = f32[128,128,38]{0,2,1:T(8,128)S(1)} fusion(f32[38,128,128]{1,0,2:T(8,128)S(1)} %bitcast_subtract_fusion.4, f32[38,38]{1,0:T(8,128)S(1)} %copy-done), kind=kOutput, calls=%fused_computation.111 | convolution fusion | flops 283901952 | bytes 4986512 | tf_op jit(solution)/shard_map/dot_general | solution.py:89
  93.1 4.5 %bitcast_subtract_fusion.2 = f32[38,128,128]{1,0,2:T(8,128)S(1)} fusion(f32[38,128,128]{1,0,2:T(8,128)S(1)} %bitcast_subtract_fusion.4, f32[128,128,38]{0,2,1:T(8,128)S(1)} %fusion.76, f32[38,128,128]{1,0,2:T(8,128)S(1)} %fusion.44, f32[128,128]{0,1:T(8,128)S(1)} %copy.76, f32[38,38]{1,0:T(8,128)S(1)} %copy-done.5), kind=kOutput, calls=%fused_computation.69 | convolution fusion | flops 290127872 | bytes 10032784 | tf_op jit(solution)/shard_map/dot_general | solution.py:96
  97.6 2.3 %fusion.74 = f32[128,128,38]{0,2,1:T(8,128)S(1)} fusion(f32[38,128,128]{1,0,2:T(8,128)S(1)} %bitcast_subtract_fusion.2, f32[38,38]{1,0:T(8,128)S(1)} %copy-done), kind=kOutput, calls=%fused_computation.109 | convolution fusion | flops 283901952 | bytes 4986512 | tf_op jit(solution)/shard_map/dot_general | solution.py:89
  99.9 4.4 %fusion.45 = f32[38,128,128]{1,0,2:T(8,128)S(1)} fusion(f32[38,128,128]{1,0,2:T(8,128)S(1)} %fusion.44, f32[38,128,128]{1,0,2:T(8,128)S(1)} %bitcast_subtract_fusion.2, f32[128,128,38]{0,2,1:T(8,128)S(1)} %fusion.74, f32[128,128]{0,1:T(8,128)S(1)} %copy.76, pred[128]{0:T(512)(128)(4,1)S(1)} %gt.22, f32[38,38]{1,0:T(8,128)S(1)} %copy-done.5), kind=kOutput, calls=%fused_computation.65 | convolution fusion | flops 290750464 | bytes 10032912 | tf_op jit(solution)/shard_map/dot_general | solution.py:96
  104.3 1.7 %convolution_bitcast_fusion = f32[4,128,128]{1,0,2:T(4,128)S(1)} fusion(f32[38,128,128]{1,0,2:T(8,128)S(1)} %fusion.45, f32[4,38]{1,0:T(4,128)S(1)} %copy-done.8), kind=kOutput, calls=%fused_computation.85 | convolution fusion | flops 29884416 | bytes 2753120 | tf_op jit(solution)/shard_map/dot_general | solution.py:102
  106.3 13.0 %psum.7 = f32[4,128]{1,0:T(4,128)S(1)} all-reduce(f32[4,128]{1,0:T(4,128)S(1)} %broadcast_multiply_fusion), channel_id=1, replica_groups=mesh['axial'=8,'radial'=4] {'radial'}, use_global_device_ids=true, to_apply=%region_0.1 | all-reduce | flops 512 | bytes 4096 | tf_op jit(solution)/shard_map/psum | solution.py:141
  119.9 5.0 %all-to-all-start = ((f32[8,4,128]{2,1,0:T(4,128)}), f32[8,4,128]{2,1,0:T(4,128)S(1)}, u32[]{:S(2)}, u32[]{:S(2)}) async-start(f32[8,4,128]{2,1,0:T(4,128)} %stack.2), calls=%async_computation | async-start | bytes 32768 | tf_op jit(solution)/shard_map/all_to_all | solution.py:143
  124.9 0.7 fusion.80
  125.6 3.4 %copy.77 = f32[38,128,128]{2,1,0:T(8,128)} copy(f32[38,128,128]{1,0,2:T(8,128)} %copy-done.3) | data formatting | bytes 4980736
  129.0 0.7 all-to-all-done
  129.6 35.0 %gather_fusion = f32[4096]{0:T(1024)S(1)} fusion(f32[4,1024]{1,0:T(4,128)S(1)} %bitcast.95, s32[4096]{0:T(1024)S(1)} %bitcast.96), kind=kCustom, calls=%fused_computation | custom fusion | bytes 65536 | tf_op jit(solution)/shard_map/jit(take_along_axis)/gather | solution.py:150
  164.6 1.3 select_subtract_fusion
  (41 shorter events, 2.6 us)
Async XLA Ops:
  0.6 83.4 %copy-start = (f32[38,38]{1,0:T(8,128)S(1)}, f32[38,38]{1,0:T(8,128)}, u32[]{:S(2)}) copy-start(f32[38,38]{1,0:T(8,128)} %param.13) | copy-start | bytes 17332
  0.6 2.6 %copy-start.4 = (f32[2,128,128]{2,1,0:T(8,128)S(1)}, f32[2,128,128]{2,1,0:T(8,128)}, u32[]{:S(2)}) copy-start(f32[2,128,128]{2,1,0:T(8,128)} %param.11) | copy-start | bytes 393220
  6.7 9.4 %copy-start.6 = (f32[128,128]{1,0:T(8,128)S(1)}, f32[128,128]{1,0:T(8,128)}, u32[]{:S(2)}) copy-start(f32[128,128]{1,0:T(8,128)} %param.12) | copy-start | bytes 196612
  6.7 9.5 %copy-start.10 = (s32[64,1]{0,1:T(1,128)S(1)}, s32[64,1]{0,1:T(1,128)}, u32[]{:S(2)}) copy-start(s32[64,1]{0,1:T(1,128)} %param.15) | copy-start | bytes 772
  9.3 7.3 %collective-permute-start.1 = (f32[40,3,128]{2,0,1:T(8,128)S(1)}, f32[40,3,128]{2,0,1:T(8,128)S(1)}, u32[]{:S(2)}, u32[]{:S(2)}) collective-permute-start(f32[40,3,128]{2,0,1:T(8,128)S(1)} %copy.67), channel_id=1, source_target_pairs={{4,0},{8,4},{12,8},{16,12},{20,16},{24,20},{28,24},{5,1},{9,5},{13... | collective-permute-start | bytes 184328 | tf_op jit(solution)/shard_map/ppermute | solution.py:24
  13.1 5.8 %collective-permute-start = (f32[40,3,128]{2,0,1:T(8,128)S(1)}, f32[40,3,128]{2,0,1:T(8,128)S(1)}, u32[]{:S(2)}, u32[]{:S(2)}) collective-permute-start(f32[40,3,128]{2,0,1:T(8,128)S(1)} %copy.65), channel_id=1, source_target_pairs={{0,4},{4,8},{8,12},{12,16},{16,20},{20,24},{24,28},{1,5},{5,9},{9,... | collective-permute-start | bytes 184328 | tf_op jit(solution)/shard_map/ppermute | solution.py:23
  21.2 1.9 %copy-start.1 = (f32[40,3,128]{1,0,2:T(8,128)S(1)}, f32[40,3,128]{1,0,2:T(8,128)}, u32[]{:S(2)}) copy-start(f32[40,3,128]{1,0,2:T(8,128)} %copy.68) | copy-start | bytes 184324
  21.2 2.6 %copy-start.2 = (f32[40,3,128]{1,0,2:T(8,128)S(1)}, f32[40,3,128]{1,0,2:T(8,128)}, u32[]{:S(2)}) copy-start(f32[40,3,128]{1,0,2:T(8,128)} %copy.66) | copy-start | bytes 184324
  27.3 31.9 %collective-permute-start.2 = (f32[40,134,3]{1,0,2:T(8,128)S(1)}, f32[40,134,3]{1,0,2:T(8,128)S(1)}, u32[]{:S(2)}, u32[]{:S(2)}) collective-permute-start(f32[40,134,3]{1,0,2:T(8,128)S(1)} %get-tuple-element.20), channel_id=1, source_target_pairs={{0,1},{1,2},{2,3},{4,5},{5,6},{6,7},{8,9},{9,10},{10,11},{12,13},{... | collective-permute-start | bytes 192968 | tf_op jit(solution)/shard_map/ppermute | solution.py:23
  32.2 26.9 %collective-permute-start.3 = (f32[40,134,3]{1,0,2:T(8,128)S(1)}, f32[40,134,3]{1,0,2:T(8,128)S(1)}, u32[]{:S(2)}, u32[]{:S(2)}) collective-permute-start(f32[40,134,3]{1,0,2:T(8,128)S(1)} %get-tuple-element.21), channel_id=1, source_target_pairs={{1,0},{2,1},{3,2},{5,4},{6,5},{7,6},{9,8},{10,9},{11,10},{13,12},{... | collective-permute-start | bytes 192968 | tf_op jit(solution)/shard_map/ppermute | solution.py:24
  84.1 2.5 %copy-start.5 = (f32[38,38]{1,0:T(8,128)S(1)}, f32[38,38]{1,0:T(8,128)}, u32[]{:S(2)}) copy-start(f32[38,38]{1,0:T(8,128)} %param.14) | copy-start | bytes 17332
  99.9 4.4 %copy-start.8 = (f32[4,38]{1,0:T(4,128)S(1)}, f32[4,38]{1,0:T(4,128)}, u32[]{:S(2)}) copy-start(f32[4,38]{1,0:T(4,128)} %param.16) | copy-start | bytes 1828
  104.3 15.6 %copy-start.3 = (f32[38,128,128]{1,0,2:T(8,128)}, f32[38,128,128]{1,0,2:T(8,128)S(1)}, u32[]{:S(2)}) copy-start(f32[38,128,128]{1,0,2:T(8,128)S(1)} %fusion.45) | copy-start | bytes 7471108
  104.3 1.7 %copy-start.9 = (f32[128]{0:T(128)S(1)}, f32[128]{0:T(128)}, u32[]{:S(2)}) copy-start(f32[128]{0:T(128)} %param.17) | copy-start | bytes 1540
  119.9 9.7 %all-to-all-start = ((f32[8,4,128]{2,1,0:T(4,128)}), f32[8,4,128]{2,1,0:T(4,128)S(1)}, u32[]{:S(2)}, u32[]{:S(2)}) async-start(f32[8,4,128]{2,1,0:T(4,128)} %stack.2), calls=%async_computation | async-start | bytes 32768 | tf_op jit(solution)/shard_map/all_to_all | solution.py:143
  129.6 35.0 %copy-start.7 = (f32[4,1024]{1,0:T(4,128)S(1)}, f32[4,1024]{1,0:T(4,128)}, u32[]{:S(2)}) copy-start(f32[4,1024]{1,0:T(4,128)} %param.19) | copy-start | bytes 49156
